TPU v7x, 256 devices: a whole 4x4x8 slice. The times are simulated.
256 devices in a mesh: win: 8 (over y, core), chan: 32 (over x, z).
Axes of the slice: x: 4, y: 4, z: 8, core: 2. Of those that a mesh axis runs over, the one named last changes fastest.
Arguments:
- traces: float32 [8, 15000, 4096], P('win', None, 'chan'), may hold values from -200 to 200
- pair_blocks: int32 [192, 2], P('chan'), may hold values from -1 to 31, as said below
Outputs:
- stacks: float32 [192, 512, 128], P('chan', 'win')
Inputs may be any that keep to these rules, and one draw needn't show every extreme that they name: `pair_blocks`: owner o holds rows o * 6 to (o + 1) * 6 - 1. Each row is a block pair (i, i + d) with 1 <= d <= 3, or (-1, -1) for an empty slot; every block pair with an offset in that range stands in exactly one row; some owner has all 6 of its slots filled.
All inputs are finite; a program needn't handle non-finite values.
Results may differ from a plain program's by a relative error of at most 0.003.
Values may be sent and summed in bfloat16 or wider, within the bound.
No kernel may reach another device: no remote copies, remote signals or barrier semaphores. Data moves between devices by JAX's collectives and lax.ppermute only.
A program may use at most 64 MiB of HBM per device.

v0:
```python
import math
import jax
import jax.numpy as jnp
from jax import lax
from jax.sharding import PartitionSpec as P

L = 15000
NB = 512
F_LO = 64
HALF = 32
LAGS = 512
two_pi = 2.0 * math.pi


def band_tables():
    width = NB + 2 * HALF
    rows = lax.broadcasted_iota(jnp.int32, (NB, width), 0)
    cols = lax.broadcasted_iota(jnp.int32, (NB, width), 1)
    smoother = jnp.where(
        (cols >= rows) & (cols <= rows + 2 * HALF), 1.0 / (2 * HALF + 1), 0.0
    ).astype(jnp.float32)
    taper = jnp.sin(
        math.pi * (lax.broadcasted_iota(jnp.int32, (NB,), 0).astype(jnp.float32) + 0.5) / NB
    )
    bins = F_LO + lax.broadcasted_iota(jnp.int32, (LAGS, NB), 1)
    lagged = lax.broadcasted_iota(jnp.int32, (LAGS, NB), 0) - LAGS // 2
    angle = (bins * lagged % L).astype(jnp.float32) * (two_pi / L)
    table = jnp.stack([jnp.cos(angle), -jnp.sin(angle)], axis=1).astype(jnp.bfloat16)
    return (smoother, taper, table)


def whiten_local(traces, smoother, taper):
    width = NB + 2 * HALF
    windows, total, channels = traces.shape
    block = math.gcd(total, 3000)

    def add_block(index, acc):
        start = index * block
        piece = lax.dynamic_slice_in_dim(traces, start, block, 1)
        bins = F_LO - HALF + lax.broadcasted_iota(jnp.int32, (width, block), 0)
        times = start + lax.broadcasted_iota(jnp.int32, (width, block), 1)
        angle = (bins * times % total).astype(jnp.float32) * (two_pi / total)
        basis = jnp.concatenate([jnp.cos(angle), -jnp.sin(angle)], axis=0)
        return acc + jnp.einsum(
            "qn,wnc->wqc",
            basis,
            piece,
            precision=lax.Precision.HIGHEST,
            preferred_element_type=jnp.float32,
        )

    spec = lax.fori_loop(
        0, total // block, add_block, jnp.zeros((windows, 2 * width, channels), jnp.float32)
    )
    real = spec[:, :width]
    imag = spec[:, width:]
    power = real * real + imag * imag
    level = jnp.einsum("bm,wmc->wbc", smoother, power, precision=lax.Precision.HIGHEST) + 1e-06
    factor = taper[None, :, None] * lax.rsqrt(level)
    white = jnp.stack(
        [real[:, HALF : HALF + NB] * factor, imag[:, HALF : HALF + NB] * factor], axis=1
    )
    return white.astype(jnp.bfloat16)


def cross_spectra(left, right):
    left_re = left[..., 0, :, :].astype(jnp.float32)
    left_im = left[..., 1, :, :].astype(jnp.float32)
    right_re = right[..., 0, :, :].astype(jnp.float32)
    right_im = right[..., 1, :, :].astype(jnp.float32)
    real = left_re * right_re + left_im * right_im
    imag = left_im * right_re - left_re * right_im
    return jnp.stack([real, imag], axis=-3).astype(jnp.bfloat16)


def correlate(cross, table, factor):
    return jnp.einsum("tqb,swqbk->stk", table, cross, preferred_element_type=jnp.float32) * factor


def body(traces, pair_blocks):
    smoother, taper, table = band_tables()
    white = whiten_local(traces, smoother, taper)
    windows_all = traces.shape[0] * lax.axis_size("win")
    factor = 1.0 / math.sqrt(NB * windows_all)
    filled = (pair_blocks[:, 0] >= 0)[:, None, None]
    every = lax.all_gather(white[None], "chan", axis=0, tiled=True)
    left_index = jnp.maximum(pair_blocks[:, 0], 0)
    right_index = jnp.maximum(pair_blocks[:, 1], 0)
    cross = cross_spectra(jnp.take(every, left_index, axis=0), jnp.take(every, right_index, axis=0))
    local = correlate(cross, table, factor)
    local = jnp.where(filled, local, 0.0)
    return lax.psum_scatter(local, "win", scatter_dimension=1, tiled=True)


def solution(mesh):
    in_specs = (P("win", None, "chan"), P("chan", None))
    out_specs = P("chan", "win", None)
    return jax.shard_map(body, mesh=mesh, in_specs=in_specs, out_specs=out_specs, check_vma=False)
```

profile of v0, /device:TPU:6, one launch (start us, length us, event | category | flops | bytes accessed | tf_op | source)
XLA Modules:
  0.0 422.1 jit_solution(8498667945533063919)
XLA Ops:
  6.6 253.2 %while.16 = (s32[]{:T(128)}, f32[1,1152,128]{1,2,0:T(8,128)S(1)}, f32[1,15000,128]{2,1,0:T(8,128)}, s32[]{:T(128)}, s32[]{:T(128)}, /*index=5*/s32[]{:T(128)}, s32[]{:T(128)}) while((s32[]{:T(128)}, f32[1,1152,128]{1,2,0:T(8,128)S(1)}, f32[1,15000,128]{2,1,0:T(8,128)}, s32[]{:T(128)}, s32[]{:T(128)}, /*index=5*/s32[]{:T(128)}, ...), condition=%wide.region_1.2_spmd.clone, body=%wide.region_0.1_spmd.clone.sunk | while | flops 5329450496 | bytes 30724180 | solution.py:52
  6.6 30.7 %fusion.84 = (f32[576,3000]{1,0:T(8,128)}, f32[576,3000]{1,0:T(8,128)}) fusion(s32[3000]{0:T(1024)S(1)} %iota_add_fusion.6, s32[576]{0:T(1024)S(1)} %iota_add_fusion.7), kind=kLoop, calls=%fused_computation.13.clone.1 | loop fusion | flops 17280000 | bytes 13838304 | tf_op jit(solution)/shard_map/while/body/eval_jaxpr/cos | solution.py:43
  37.4 19.8 %fusion.85 = f32[1,1152,128]{1,2,0:T(8,128)S(1)} fusion(f32[576,3000]{1,0:T(8,128)} %get-tuple-element.151, f32[576,3000]{1,0:T(8,128)} %get-tuple-element.152, f32[1,15000,128]{2,1,0:T(8,128)} %get-tuple-element.169, s32[]{:T(128)S(6)} %select_n.131, f32[1,1152,128]{1,2,0:T(8,128)S(1)} %get-tuple-element.161, pred[]{:T(512)S(6)} %compare.3), kind=kOutput, calls=%fused_computation.16.clone.1 | convolution fusion | flops 5312166912 | bytes 16871428 | tf_op jit(solution)/shard_map/while/body/eval_jaxpr/qn,wnc->wqc/dot_general | solution.py:44
  57.2 30.7 %fusion.84 = (f32[576,3000]{1,0:T(8,128)}, f32[576,3000]{1,0:T(8,128)}) fusion(s32[3000]{0:T(1024)S(1)} %iota_add_fusion.6, s32[576]{0:T(1024)S(1)} %iota_add_fusion.7), kind=kLoop, calls=%fused_computation.13.clone.1 | loop fusion | flops 17280000 | bytes 13838304 | tf_op jit(solution)/shard_map/while/body/eval_jaxpr/cos | solution.py:43
  88.0 19.8 %fusion.85 = f32[1,1152,128]{1,2,0:T(8,128)S(1)} fusion(f32[576,3000]{1,0:T(8,128)} %get-tuple-element.151, f32[576,3000]{1,0:T(8,128)} %get-tuple-element.152, f32[1,15000,128]{2,1,0:T(8,128)} %get-tuple-element.169, s32[]{:T(128)S(6)} %select_n.131, f32[1,1152,128]{1,2,0:T(8,128)S(1)} %get-tuple-element.161, pred[]{:T(512)S(6)} %compare.3), kind=kOutput, calls=%fused_computation.16.clone.1 | convolution fusion | flops 5312166912 | bytes 16871428 | tf_op jit(solution)/shard_map/while/body/eval_jaxpr/qn,wnc->wqc/dot_general | solution.py:44
  107.8 30.7 %fusion.84 = (f32[576,3000]{1,0:T(8,128)}, f32[576,3000]{1,0:T(8,128)}) fusion(s32[3000]{0:T(1024)S(1)} %iota_add_fusion.6, s32[576]{0:T(1024)S(1)} %iota_add_fusion.7), kind=kLoop, calls=%fused_computation.13.clone.1 | loop fusion | flops 17280000 | bytes 13838304 | tf_op jit(solution)/shard_map/while/body/eval_jaxpr/cos | solution.py:43
  138.6 19.8 %fusion.85 = f32[1,1152,128]{1,2,0:T(8,128)S(1)} fusion(f32[576,3000]{1,0:T(8,128)} %get-tuple-element.151, f32[576,3000]{1,0:T(8,128)} %get-tuple-element.152, f32[1,15000,128]{2,1,0:T(8,128)} %get-tuple-element.169, s32[]{:T(128)S(6)} %select_n.131, f32[1,1152,128]{1,2,0:T(8,128)S(1)} %get-tuple-element.161, pred[]{:T(512)S(6)} %compare.3), kind=kOutput, calls=%fused_computation.16.clone.1 | convolution fusion | flops 5312166912 | bytes 16871428 | tf_op jit(solution)/shard_map/while/body/eval_jaxpr/qn,wnc->wqc/dot_general | solution.py:44
  158.4 30.7 %fusion.84 = (f32[576,3000]{1,0:T(8,128)}, f32[576,3000]{1,0:T(8,128)}) fusion(s32[3000]{0:T(1024)S(1)} %iota_add_fusion.6, s32[576]{0:T(1024)S(1)} %iota_add_fusion.7), kind=kLoop, calls=%fused_computation.13.clone.1 | loop fusion | flops 17280000 | bytes 13838304 | tf_op jit(solution)/shard_map/while/body/eval_jaxpr/cos | solution.py:43
  189.2 19.8 %fusion.85 = f32[1,1152,128]{1,2,0:T(8,128)S(1)} fusion(f32[576,3000]{1,0:T(8,128)} %get-tuple-element.151, f32[576,3000]{1,0:T(8,128)} %get-tuple-element.152, f32[1,15000,128]{2,1,0:T(8,128)} %get-tuple-element.169, s32[]{:T(128)S(6)} %select_n.131, f32[1,1152,128]{1,2,0:T(8,128)S(1)} %get-tuple-element.161, pred[]{:T(512)S(6)} %compare.3), kind=kOutput, calls=%fused_computation.16.clone.1 | convolution fusion | flops 5312166912 | bytes 16871428 | tf_op jit(solution)/shard_map/while/body/eval_jaxpr/qn,wnc->wqc/dot_general | solution.py:44
  209.0 30.7 %fusion.84 = (f32[576,3000]{1,0:T(8,128)}, f32[576,3000]{1,0:T(8,128)}) fusion(s32[3000]{0:T(1024)S(1)} %iota_add_fusion.6, s32[576]{0:T(1024)S(1)} %iota_add_fusion.7), kind=kLoop, calls=%fused_computation.13.clone.1 | loop fusion | flops 17280000 | bytes 13838304 | tf_op jit(solution)/shard_map/while/body/eval_jaxpr/cos | solution.py:43
  239.8 19.8 %fusion.85 = f32[1,1152,128]{1,2,0:T(8,128)S(1)} fusion(f32[576,3000]{1,0:T(8,128)} %get-tuple-element.151, f32[576,3000]{1,0:T(8,128)} %get-tuple-element.152, f32[1,15000,128]{2,1,0:T(8,128)} %get-tuple-element.169, s32[]{:T(128)S(6)} %select_n.131, f32[1,1152,128]{1,2,0:T(8,128)S(1)} %get-tuple-element.161, pred[]{:T(512)S(6)} %compare.3), kind=kOutput, calls=%fused_computation.16.clone.1 | convolution fusion | flops 5312166912 | bytes 16871428 | tf_op jit(solution)/shard_map/while/body/eval_jaxpr/qn,wnc->wqc/dot_general | solution.py:44
  259.8 0.0 copy-start.2
  259.8 1.4 fusion.69
  261.3 0.8 copy.21
  262.1 0.0 all-gather.2.cloned.1.call-update
  262.1 0.0 reduce-scatter.2.cloned.1.call-start
  262.3 5.7 %cosine_convert_fusion = (bf16[512,1,512]{2,0,1:T(8,128)(2,1)}, bf16[512,1,512]{2,0,1:T(8,128)(2,1)}) fusion(s32[512]{0:T(512)S(1)} %iota_add_fusion.2, s32[512]{0:T(512)S(1)} %iota_add_fusion.3), kind=kLoop, calls=%fused_computation.57 | loop fusion | flops 3145728 | bytes 1052672 | tf_op jit(solution)/shard_map/convert
  268.0 93.6 %all-gather.2.cloned.1.call-done = bf16[32,1,2,512,128]{4,3,2,1,0:T(8,128)(2,1)} async-done(((bf16[1,1,2,512,128]{4,3,2,1,0:T(8,128)(2,1)}), bf16[32,1,2,512,128]{4,3,2,1,0:T(8,128)(2,1)}) %all-gather.2.cloned.1.call-update) | async-done | bytes 8388624 | tf_op jit(solution)/shard_map/all_gather | solution.py:86
  361.6 4.2 %gather_fusion.1 = bf16[6,2,512,128]{3,2,1,0:T(8,128)(2,1)S(1)} fusion(bf16[32,2,512,128]{3,2,1,0:T(8,128)(2,1)} %bitcast.65, s32[1024]{0:T(1024)S(1)} %pad_clamp_fusion), kind=kCustom, calls=%fused_computation.1.clone | custom fusion | bytes 3145752 | tf_op jit(solution)/shard_map/jit(_take)/gather | solution.py:89
  365.9 0.7 copy.23
  366.6 4.2 %gather_fusion = bf16[6,2,512,128]{3,2,1,0:T(8,128)(2,1)S(1)} fusion(bf16[32,2,512,128]{3,2,1,0:T(8,128)(2,1)} %bitcast.66, s32[1024]{0:T(1024)S(1)} %pad_clamp_fusion.1), kind=kCustom, calls=%fused_computation.clone | custom fusion | bytes 3145752 | tf_op jit(solution)/shard_map/jit(_take)/gather | solution.py:89
  370.8 1.6 copy.22
  372.4 1.7 bitcast_select_fusion
  374.2 0.0 copy-start
  374.2 0.6 fusion.59
  374.8 0.4 copy-done
  375.2 0.2 copy-done.1
  375.4 1.0 fusion.29
  376.4 1.8 copy.24
  378.2 0.0 reduce-scatter.2.cloned.1.call-update
  378.2 35.3 %reduce-scatter.2.cloned.1.call-done = f32[6,64,128]{2,0,1:T(8,128)} async-done(((f32[6,512,128]{2,0,1:T(8,128)}), f32[6,64,128]{2,0,1:T(8,128)}) %reduce-scatter.2.cloned.1.call-update) | async-done | bytes 196624 | tf_op jit(solution)/shard_map/reduce_scatter | solution.py:92
  413.6 1.7 copy.25
  (22 shorter events, 0.2 us)
Async XLA Ops:
  6.5 355.1 %all-gather.2.cloned.1.call-start = ((), (), s32[]{:S(2)}) async-start(), calls=%async_computation.1 | async-start | bytes 8650752 | tf_op jit(solution)/shard_map/all_gather | solution.py:86
  259.8 2.4 copy-start.2
  262.1 151.4 %reduce-scatter.2.cloned.1.call-start = ((), (), s32[]{:S(2)}) async-start(), calls=%async_computation.2 | async-start | bytes 2359296 | tf_op jit(solution)/shard_map/reduce_scatter | solution.py:92
  374.2 1.0 copy-start
  374.2 1.2 copy-start.1
Sparse Core Ops, SparseCore 0:
  262.2 99.3 all-gather.1
  378.4 35.1 reduce-scatter.1
where the time goes:
time: 422 us
  other arithmetic  162 us (38%)
  waiting for transfers between devices  129 us (31%)
  matrix products  101 us (24%)
  local copies, waits for them, and re-layouts  15.7 us (4%)
  between operations  13.5 us (3%)
    cos x5, other arithmetic, add_block(): basis = jnp.concatenate([jnp.cos(angle), -jnp.sin(angle)], axis=0)  154 us
    dot_general x5, matrix products, add_block(): jnp.einsum('qn,wnc->wqc', basis, piece, precision=lax.Precision.HIGHEST,...  99.1 us
    all_gather x1, waiting for transfers between devices, body(): every = lax.all_gather(white[None], 'chan', axis=0, tiled=True)  93.6 us
    reduce_scatter x1, waiting for transfers between devices, body(): return lax.psum_scatter(local, 'win', scatter_dimension=1, tiled=True)  35.3 us
  transfers between devices with their start and end apart: 2, of which 2 were waited for; matrix products, arithmetic and copies ran while one was open for 1% of the time, Pallas kernels for 0%

commit v1 on v0

--- a/solution.py
+++ b/solution.py
@@ -3,6 +3,7 @@
 import jax.numpy as jnp
 from jax import lax
 from jax.sharding import PartitionSpec as P
+from jax.lax import all_to_all, axis_size
 
 L = 15000
 NB = 512
@@ -83,7 +84,12 @@
     windows_all = traces.shape[0] * lax.axis_size("win")
     factor = 1.0 / math.sqrt(NB * windows_all)
     filled = (pair_blocks[:, 0] >= 0)[:, None, None]
-    every = lax.all_gather(white[None], "chan", axis=0, tiled=True)
+    every = jnp.concatenate(
+        all_to_all(
+            jnp.stack([white[None]] * axis_size("chan"), 0), "chan", split_axis=0, concat_axis=0
+        ),
+        0,
+    )
     left_index = jnp.maximum(pair_blocks[:, 0], 0)
     right_index = jnp.maximum(pair_blocks[:, 1], 0)
     cross = cross_spectra(jnp.take(every, left_index, axis=0), jnp.take(every, right_index, axis=0))

time: 422 us -> 535 us (1.27)
  waiting for transfers between devices: 129 us -> 225 us
  starting transfers between devices: 0.04 us -> 11.8 us
    all_to_all x0 -> x1, waiting for transfers between devices: none -> 186 us  [body(): all_to_all(jnp.stack([white[None]] * axis_size('chan'), 0), 'chan', split...]
    all_gather x1 -> x0, waiting for transfers between devices: 93.6 us -> none  [body(): every = lax.all_gather(white[None], 'chan', axis=0, tiled=True)]
    all_to_all x0 -> x1, starting transfers between devices: none -> 11.8 us  [body(): all_to_all(jnp.stack([white[None]] * axis_size('chan'), 0), 'chan', split...]
where the time goes in v1:
time: 535 us; the launch traced here: 534 us
  waiting for transfers between devices  225 us (42%)
  other arithmetic  162 us (30%)
  matrix products  102 us (19%)
  local copies, waits for them, and re-layouts  20.2 us (4%)
  between operations  13.5 us (3%)
  starting transfers between devices  11.8 us (2%)
    all_to_all x1, waiting for transfers between devices, body(): all_to_all(jnp.stack([white[None]] * axis_size('chan'), 0), 'chan', split...  186 us
    cos x5, other arithmetic, add_block(): basis = jnp.concatenate([jnp.cos(angle), -jnp.sin(angle)], axis=0)  154 us
    dot_general x5, matrix products, add_block(): jnp.einsum('qn,wnc->wqc', basis, piece, precision=lax.Precision.HIGHEST,...  99.1 us
    reduce_scatter x1, waiting for transfers between devices, body(): return lax.psum_scatter(local, 'win', scatter_dimension=1, tiled=True)  38.3 us
    all_to_all x1, starting transfers between devices, body(): all_to_all(jnp.stack([white[None]] * axis_size('chan'), 0), 'chan', split...  11.8 us
  transfers between devices with their start and end apart: 2, of which 2 were waited for; matrix products, arithmetic and copies ran while one was open for 1% of the time, Pallas kernels for 0%

profile of v1, /device:TPU:6, one launch (start us, length us, event | category | flops | bytes accessed | tf_op | source)
XLA Modules:
  0.0 534.2 jit_solution(14280153449140302995)
XLA Ops:
  6.6 253.3 %while.16 = (s32[]{:T(128)}, f32[1,1152,128]{1,2,0:T(8,128)S(1)}, f32[1,15000,128]{2,1,0:T(8,128)}, s32[]{:T(128)}, s32[]{:T(128)}, /*index=5*/s32[]{:T(128)}, s32[]{:T(128)}) while((s32[]{:T(128)}, f32[1,1152,128]{1,2,0:T(8,128)S(1)}, f32[1,15000,128]{2,1,0:T(8,128)}, s32[]{:T(128)}, s32[]{:T(128)}, /*index=5*/s32[]{:T(128)}, ...), condition=%wide.region_1.2_spmd.clone, body=%wide.region_0.1_spmd.clone.sunk | while | flops 5329450496 | bytes 30724172 | solution.py:53
  6.6 30.8 %fusion.78 = (f32[576,3000]{1,0:T(8,128)}, f32[576,3000]{1,0:T(8,128)}) fusion(s32[3000]{0:T(1024)S(1)} %iota_add_fusion.6, s32[576]{0:T(1024)S(1)} %iota_add_fusion.7), kind=kLoop, calls=%fused_computation.13.clone.1 | loop fusion | flops 17280000 | bytes 13838304 | tf_op jit(solution)/shard_map/while/body/eval_jaxpr/cos | solution.py:44
  37.4 19.8 %fusion.79 = f32[1,1152,128]{1,2,0:T(8,128)S(1)} fusion(f32[576,3000]{1,0:T(8,128)} %get-tuple-element.151, f32[576,3000]{1,0:T(8,128)} %get-tuple-element.152, f32[1,15000,128]{2,1,0:T(8,128)} %get-tuple-element.169, s32[]{:T(128)S(6)} %select_n.131, f32[1,1152,128]{1,2,0:T(8,128)S(1)} %get-tuple-element.161, pred[]{:T(512)S(6)} %compare.3), kind=kOutput, calls=%fused_computation.16.clone.1 | convolution fusion | flops 5312166912 | bytes 16871428 | tf_op jit(solution)/shard_map/while/body/eval_jaxpr/qn,wnc->wqc/dot_general | solution.py:45
  57.2 30.8 %fusion.78 = (f32[576,3000]{1,0:T(8,128)}, f32[576,3000]{1,0:T(8,128)}) fusion(s32[3000]{0:T(1024)S(1)} %iota_add_fusion.6, s32[576]{0:T(1024)S(1)} %iota_add_fusion.7), kind=kLoop, calls=%fused_computation.13.clone.1 | loop fusion | flops 17280000 | bytes 13838304 | tf_op jit(solution)/shard_map/while/body/eval_jaxpr/cos | solution.py:44
  88.0 19.8 %fusion.79 = f32[1,1152,128]{1,2,0:T(8,128)S(1)} fusion(f32[576,3000]{1,0:T(8,128)} %get-tuple-element.151, f32[576,3000]{1,0:T(8,128)} %get-tuple-element.152, f32[1,15000,128]{2,1,0:T(8,128)} %get-tuple-element.169, s32[]{:T(128)S(6)} %select_n.131, f32[1,1152,128]{1,2,0:T(8,128)S(1)} %get-tuple-element.161, pred[]{:T(512)S(6)} %compare.3), kind=kOutput, calls=%fused_computation.16.clone.1 | convolution fusion | flops 5312166912 | bytes 16871428 | tf_op jit(solution)/shard_map/while/body/eval_jaxpr/qn,wnc->wqc/dot_general | solution.py:45
  107.9 30.8 %fusion.78 = (f32[576,3000]{1,0:T(8,128)}, f32[576,3000]{1,0:T(8,128)}) fusion(s32[3000]{0:T(1024)S(1)} %iota_add_fusion.6, s32[576]{0:T(1024)S(1)} %iota_add_fusion.7), kind=kLoop, calls=%fused_computation.13.clone.1 | loop fusion | flops 17280000 | bytes 13838304 | tf_op jit(solution)/shard_map/while/body/eval_jaxpr/cos | solution.py:44
  138.6 19.8 %fusion.79 = f32[1,1152,128]{1,2,0:T(8,128)S(1)} fusion(f32[576,3000]{1,0:T(8,128)} %get-tuple-element.151, f32[576,3000]{1,0:T(8,128)} %get-tuple-element.152, f32[1,15000,128]{2,1,0:T(8,128)} %get-tuple-element.169, s32[]{:T(128)S(6)} %select_n.131, f32[1,1152,128]{1,2,0:T(8,128)S(1)} %get-tuple-element.161, pred[]{:T(512)S(6)} %compare.3), kind=kOutput, calls=%fused_computation.16.clone.1 | convolution fusion | flops 5312166912 | bytes 16871428 | tf_op jit(solution)/shard_map/while/body/eval_jaxpr/qn,wnc->wqc/dot_general | solution.py:45
  158.5 30.8 %fusion.78 = (f32[576,3000]{1,0:T(8,128)}, f32[576,3000]{1,0:T(8,128)}) fusion(s32[3000]{0:T(1024)S(1)} %iota_add_fusion.6, s32[576]{0:T(1024)S(1)} %iota_add_fusion.7), kind=kLoop, calls=%fused_computation.13.clone.1 | loop fusion | flops 17280000 | bytes 13838304 | tf_op jit(solution)/shard_map/while/body/eval_jaxpr/cos | solution.py:44
  189.2 19.8 %fusion.79 = f32[1,1152,128]{1,2,0:T(8,128)S(1)} fusion(f32[576,3000]{1,0:T(8,128)} %get-tuple-element.151, f32[576,3000]{1,0:T(8,128)} %get-tuple-element.152, f32[1,15000,128]{2,1,0:T(8,128)} %get-tuple-element.169, s32[]{:T(128)S(6)} %select_n.131, f32[1,1152,128]{1,2,0:T(8,128)S(1)} %get-tuple-element.161, pred[]{:T(512)S(6)} %compare.3), kind=kOutput, calls=%fused_computation.16.clone.1 | convolution fusion | flops 5312166912 | bytes 16871428 | tf_op jit(solution)/shard_map/while/body/eval_jaxpr/qn,wnc->wqc/dot_general | solution.py:45
  209.1 30.8 %fusion.78 = (f32[576,3000]{1,0:T(8,128)}, f32[576,3000]{1,0:T(8,128)}) fusion(s32[3000]{0:T(1024)S(1)} %iota_add_fusion.6, s32[576]{0:T(1024)S(1)} %iota_add_fusion.7), kind=kLoop, calls=%fused_computation.13.clone.1 | loop fusion | flops 17280000 | bytes 13838304 | tf_op jit(solution)/shard_map/while/body/eval_jaxpr/cos | solution.py:44
  239.9 19.8 %fusion.79 = f32[1,1152,128]{1,2,0:T(8,128)S(1)} fusion(f32[576,3000]{1,0:T(8,128)} %get-tuple-element.151, f32[576,3000]{1,0:T(8,128)} %get-tuple-element.152, f32[1,15000,128]{2,1,0:T(8,128)} %get-tuple-element.169, s32[]{:T(128)S(6)} %select_n.131, f32[1,1152,128]{1,2,0:T(8,128)S(1)} %get-tuple-element.161, pred[]{:T(512)S(6)} %compare.3), kind=kOutput, calls=%fused_computation.16.clone.1 | convolution fusion | flops 5312166912 | bytes 16871428 | tf_op jit(solution)/shard_map/while/body/eval_jaxpr/qn,wnc->wqc/dot_general | solution.py:45
  259.9 1.4 multiply_convert_fusion.1
  261.3 0.2 copy.11
  261.5 5.3 stack.24
  266.8 11.8 %all-to-all-start = ((bf16[32,1,1,2,512,128]{5,4,3,2,1,0:T(8,128)(2,1)}), bf16[32,1,1,2,512,128]{5,4,3,2,1,0:T(8,128)(2,1)}, u32[]{:S(2)}, u32[]{:S(2)}) async-start(bf16[32,1,1,2,512,128]{5,4,3,2,1,0:T(8,128)(2,1)} %stack.24), calls=%async_computation | async-start | bytes 16777216 | tf_op jit(solution)/shard_map/all_to_all | solution.py:88
  278.6 0.0 reduce-scatter.2.cloned.1.call-start
  278.6 0.0 copy-done.2
  278.7 5.8 %cosine_convert_fusion = (bf16[512,1,512]{2,0,1:T(8,128)(2,1)}, bf16[512,1,512]{2,0,1:T(8,128)(2,1)}) fusion(s32[512]{0:T(512)S(1)} %iota_add_fusion.2, s32[512]{0:T(512)S(1)} %iota_add_fusion.3), kind=kLoop, calls=%fused_computation.57 | loop fusion | flops 3145728 | bytes 1052672 | tf_op jit(solution)/shard_map/convert
  284.5 186.3 %all-to-all-done = bf16[32,1,1,2,512,128]{5,4,3,2,1,0:T(8,128)(2,1)} async-done(((bf16[32,1,1,2,512,128]{5,4,3,2,1,0:T(8,128)(2,1)}), bf16[32,1,1,2,512,128]{5,4,3,2,1,0:T(8,128)(2,1)}, u32[]{:S(2)}, u32[]{:S(2)}) %all-to-all-start) | async-done | bytes 8388640 | tf_op jit(solution)/shard_map/all_to_all | solution.py:88
  470.8 4.2 gather_fusion
  475.1 0.7 copy.12
  475.8 4.2 gather_fusion.1
  480.0 1.6 copy.13
  481.6 1.7 bitcast_select_fusion
  483.4 0.6 fusion.59
  484.0 0.4 copy-done
  484.4 0.2 copy-done.1
  484.6 1.0 fusion.29
  485.6 1.8 copy.15
  487.4 0.0 reduce-scatter.2.cloned.1.call-update
  487.4 38.3 %reduce-scatter.2.cloned.1.call-done = f32[6,64,128]{2,0,1:T(8,128)} async-done(((f32[6,512,128]{2,0,1:T(8,128)}), f32[6,64,128]{2,0,1:T(8,128)}) %reduce-scatter.2.cloned.1.call-update) | async-done | bytes 196624 | tf_op jit(solution)/shard_map/reduce_scatter | solution.py:98
  525.7 1.7 copy.16
  (22 shorter events, 0.2 us)
Async XLA Ops:
  266.8 11.9 %copy-start.2 = (s32[6,2]{0,1:T(2,128)S(1)}, s32[6,2]{0,1:T(2,128)}, u32[]{:S(2)}) copy-start(s32[6,2]{0,1:T(2,128)} %param.7) | copy-start | bytes 148
  266.8 204.1 %all-to-all-start = ((bf16[32,1,1,2,512,128]{5,4,3,2,1,0:T(8,128)(2,1)}), bf16[32,1,1,2,512,128]{5,4,3,2,1,0:T(8,128)(2,1)}, u32[]{:S(2)}, u32[]{:S(2)}) async-start(bf16[32,1,1,2,512,128]{5,4,3,2,1,0:T(8,128)(2,1)} %stack.24), calls=%async_computation | async-start | bytes 16777216 | tf_op jit(solution)/shard_map/all_to_all | solution.py:88
  278.6 247.1 %reduce-scatter.2.cloned.1.call-start = ((), (), s32[]{:S(2)}) async-start(), calls=%async_computation.2 | async-start | bytes 2359296 | tf_op jit(solution)/shard_map/reduce_scatter | solution.py:98
  483.4 1.0 copy-start
  483.4 1.2 copy-start.1
Sparse Core Ops, SparseCore 0:
  487.6 38.1 reduce-scatter.1
